TPU v7x, 256 devices: a whole 4x4x8 slice. The times are simulated.
256 devices in a mesh: gx: 8 (over y, core), gy: 8 (over z), ba: 4 (over x).
Axes of the slice: x: 4, y: 4, z: 8, core: 2. Of those that a mesh axis runs over, the one named last changes fastest.
Arguments:
- pixels: float32 [224, 128, 1024], P('ba', 'gy', 'gx'), may hold values from -8 to 8
- spectra: float32 [224, 256], P('ba'), may hold values from -0.375 to 0.375
- abundance: float32 [256, 128, 1024], P('ba', 'gy', 'gx'), may hold values from 0 to 1
- plan: int32 [3], replicated, may hold values from 0 to 1, as said below
Outputs:
- sparse: float32 [256, 128, 1024], P('ba', 'gy', 'gx')
- spectra_grad: float32 [224, 256], P('ba')
Inputs may be any that keep to these rules, and one draw needn't show every extreme that they name: `plan`: entry 0 is 1 and at least one later entry is 0.
All inputs are finite; a program needn't handle non-finite values. Where the computation divides by a largest or mean magnitude, that divisor is 1e-20 or more.
Results may differ from a plain program's by a relative error of at most 0.0001.
Values sent between devices are 32-bit elements; how exact they have to be, the bound alone decides.
No kernel may reach another device: no remote copies, remote signals or barrier semaphores. Data moves between devices by JAX's collectives and lax.ppermute only.
A program may use at most 64 MiB of HBM per device.

v0:
```python
import math
import jax
import jax.numpy as jnp
from jax import lax
from jax.sharding import PartitionSpec as P

SWEEPS = 3
HIGHEST = lax.Precision.HIGHEST
penalty = 1.0
tv_weight = 0.2
sparsity = 0.05


def extended_2(x, sides, width):
    for axis, dim in sides:
        size, length = (lax.axis_size(axis), x.shape[dim])
        up = [(i, (i + 1) % size) for i in range(size - 1)]
        down = [(j, i) for i, j in up]
        last = lax.slice_in_dim(x, length - width, length, axis=dim)
        leading = lax.slice_in_dim(x, 0, width, axis=dim)
        before = lax.ppermute(last, axis, up)
        after = lax.ppermute(leading, axis, down)
        x = jnp.concatenate([before, x, after], axis=dim)
    return x


def edge_masks(top_row, left_col, row_count, col_count, grid_rows, grid_cols):
    ext_rows = top_row - 1 + jnp.arange(row_count + 1)
    ext_cols = left_col - 1 + jnp.arange(col_count + 1)
    rows_in = (ext_rows >= 0) & (ext_rows <= grid_rows - 1)
    cols_in = (ext_cols >= 0) & (ext_cols <= grid_cols - 1)
    rows_ok = (ext_rows >= 0) & (ext_rows <= grid_rows - 2)
    cols_ok = (ext_cols >= 0) & (ext_cols <= grid_cols - 2)
    mask_h = (rows_in[:, None] & cols_ok[None, :]).astype(jnp.float32)[None]
    mask_v = (rows_ok[:, None] & cols_in[None, :]).astype(jnp.float32)[None]
    return (mask_h, mask_v)


def local(pixels, spectra, abundance, plan):
    comp_share, row_count, gx_cols = abundance.shape
    band_ways = lax.axis_size("ba")
    grid_rows = row_count * lax.axis_size("gy")
    grid_cols = gx_cols * lax.axis_size("gx")
    all_comps = comp_share * band_ways
    top_row = lax.axis_index("gy") * row_count
    all_spectra = lax.all_gather(spectra, "ba", axis=0, tiled=True)
    first_comp = lax.axis_index("ba") * comp_share
    own_cols = lax.dynamic_slice_in_dim(all_spectra, first_comp, comp_share, 1)
    gram_rows = jnp.dot(own_cols.T, all_spectra, precision=HIGHEST)
    bound = lax.pmax(jnp.max(jnp.sum(jnp.abs(gram_rows), axis=1)), "ba")
    left_col = lax.axis_index("gx") * gx_cols
    mask_h, mask_v = edge_masks(top_row, left_col, row_count, gx_cols, grid_rows, grid_cols)
    field = abundance
    sparse = abundance
    dual = jnp.zeros_like(abundance)
    weight = jnp.ones((comp_share, row_count + 1, gx_cols + 1), jnp.float32)
    for sweep in range(SWEEPS):
        extended = extended_2(field, (("gx", 2), ("gy", 1)), 1)
        center = extended[:, : row_count + 1, : gx_cols + 1]
        right = extended[:, : row_count + 1, 1:]
        below = extended[:, 1:, : gx_cols + 1]
        diff_h = (right - center) * mask_h
        diff_v = (below - center) * mask_v
        energy = diff_h * diff_h + diff_v * diff_v
        total = lax.psum(jnp.sum(energy[:, 1:, 1:]), ("gx", "gy", "ba"))
        smooth_sq = total / (all_comps * grid_rows * grid_cols) + 1e-06
        fresh = 1.0 / jnp.sqrt(energy + smooth_sq)
        weight = jnp.where(plan[sweep] == 1, fresh, weight)
        flux_h = weight * diff_h
        flux_v = weight * diff_v
        edge_h = weight * mask_h
        edge_v = weight * mask_v
        tv_grad = flux_h[:, 1:, :-1] - flux_h[:, 1:, 1:] + flux_v[:, :-1, 1:] - flux_v[:, 1:, 1:]
        degree = edge_h[:, 1:, 1:] + edge_h[:, 1:, :-1] + edge_v[:, 1:, 1:] + edge_v[:, :-1, 1:]
        mixed = jnp.einsum(
            "lq,qrc->lrc",
            spectra,
            lax.all_gather(field, "ba", axis=0, tiled=True),
            precision=HIGHEST,
        )
        resid = mixed - pixels
        data_grad = lax.psum_scatter(
            jnp.einsum("lp,lrc->prc", spectra, resid, precision=HIGHEST),
            "ba",
            scatter_dimension=0,
            tiled=True,
        )
        grad_total = data_grad + tv_weight * tv_grad + penalty * (field - sparse + dual)
        field = field - grad_total / (bound + penalty + 2.0 * tv_weight * degree)
        sparse = jnp.maximum(field + dual - sparsity / penalty, 0.0)
        dual = dual + field - sparse
    all_sparse = lax.all_gather(sparse, "ba", axis=0, tiled=True)
    resid = jnp.einsum("lp,prc->lrc", spectra, all_sparse, precision=HIGHEST) - pixels
    partial_grad = jnp.einsum("lrc,prc->lp", resid, all_sparse, precision=HIGHEST) / math.sqrt(
        grid_rows * grid_cols
    )
    spectra_grad = lax.psum(partial_grad, ("gx", "gy"))
    return (sparse, spectra_grad)


def solution(mesh):
    return jax.shard_map(
        local,
        mesh=mesh,
        in_specs=(P("ba", "gy", "gx"), P("ba", None), P("ba", "gy", "gx"), P()),
        out_specs=(P("ba", "gy", "gx"), P("ba", None)),
        check_vma=False,
    )
```

profile of v0, /device:TPU:2, one launch (start us, length us, event | category | flops | bytes accessed | tf_op | source)
XLA Modules:
  0.0 793.5 jit_solution(9205692723680209742)
XLA Ops:
  8.0 37.2 %all-gather.5.cloned.1.call-done = f32[256,16,128]{2,1,0:T(8,128)} async-done(((f32[64,16,128]{2,1,0:T(8,128)}), f32[256,16,128]{2,1,0:T(8,128)}) %all-gather.5.cloned.1.call-update) | async-done | bytes 2097168 | tf_op jit(solution)/shard_map/all_gather | solution.py:78
  45.1 3.5 fusion.4
  50.6 2.0 copy.19
  56.8 12.2 %all_gather.16 = f32[224,256]{1,0:T(8,128)S(1)} all-gather(f32[56,256]{1,0:T(8,128)S(1)} %copy-done.14), channel_id=1, replica_groups=mesh['gx'=8,'gy'=8,'ba'=4] {'ba'}, dimensions={0}, use_global_device_ids=true | all-gather | bytes 286720 | tf_op jit(solution)/shard_map/all_gather | solution.py:46
  70.8 3.5 collective-permute-start.2
  74.9 10.9 %pmax.7 = f32[]{:T(128)} all-reduce(f32[]{:T(128)} %reduce_max.9), channel_id=1, replica_groups=mesh['gx'=8,'gy'=8,'ba'=4] {'ba'}, use_global_device_ids=true, to_apply=%region_5.6 | all-reduce | flops 1 | bytes 8 | tf_op jit(solution)/shard_map/pmax | solution.py:50
  88.5 4.2 collective-permute-done.3
  96.1 78.7 %psum.28 = f32[]{:T(128)} all-reduce(f32[]{:T(128)} %slice_reduce_fusion.2), channel_id=1, replica_groups=mesh['gx'=8,'gy'=8,'ba'=4] {'gx','gy','ba'}, use_global_device_ids=true, to_apply=%region_2.0 | all-reduce | flops 1 | bytes 8 | tf_op jit(solution)/shard_map/psum | solution.py:65
  175.5 5.1 fusion.55
  180.6 6.1 fusion.45
  187.0 30.1 %all-gather.7.cloned.1.call-done = f32[256,16,128]{2,1,0:T(8,128)} async-done(((f32[64,16,128]{2,1,0:T(8,128)}), f32[256,16,128]{2,1,0:T(8,128)}) %all-gather.7.cloned.1.call-update) | async-done | bytes 2097168 | tf_op jit(solution)/shard_map/all_gather | solution.py:78
  217.1 3.5 fusion.2
  228.9 3.7 collective-permute-done.5
  233.1 3.5 collective-permute-start.6
  239.2 3.6 collective-permute-done.7
  246.3 83.2 %psum.29 = f32[]{:T(128)} all-reduce(f32[]{:T(128)} %slice_reduce_fusion.1), channel_id=1, replica_groups=mesh['gx'=8,'gy'=8,'ba'=4] {'gx','gy','ba'}, use_global_device_ids=true, to_apply=%region_8.9 | all-reduce | flops 1 | bytes 8 | tf_op jit(solution)/shard_map/psum | solution.py:65
  330.1 3.6 fusion.56
  334.9 2.7 fusion.68
  337.6 6.1 fusion.38
  344.0 29.8 %all-gather.9.cloned.1.call-done = f32[256,16,128]{2,1,0:T(8,128)} async-done(((f32[64,16,128]{2,1,0:T(8,128)}), f32[256,16,128]{2,1,0:T(8,128)}) %all-gather.9.cloned.1.call-update) | async-done | bytes 2097168 | tf_op jit(solution)/shard_map/all_gather | solution.py:78
  373.8 3.5 fusion
  385.6 3.7 collective-permute-done.9
  389.8 3.5 collective-permute-start.10
  395.9 3.6 collective-permute-done.11
  403.0 83.4 %psum.30 = f32[]{:T(128)} all-reduce(f32[]{:T(128)} %slice_reduce_fusion), channel_id=1, replica_groups=mesh['gx'=8,'gy'=8,'ba'=4] {'gx','gy','ba'}, use_global_device_ids=true, to_apply=%region_11.12 | all-reduce | flops 1 | bytes 8 | tf_op jit(solution)/shard_map/psum | solution.py:65
  487.1 3.7 fusion.57
  490.8 2.6 fusion.69
  493.4 6.1 fusion.49
  499.6 30.1 %all-gather.11.cloned.1.call-done = f32[256,16,128]{2,1,0:T(8,128)} async-done(((f32[64,16,128]{2,1,0:T(8,128)}), f32[256,16,128]{2,1,0:T(8,128)}) %all-gather.11.cloned.1.call-update) | async-done | bytes 2097168 | tf_op jit(solution)/shard_map/all_gather | solution.py:92
  529.7 3.7 fusion.6
  533.5 2.3 fusion.22
  535.8 250.9 %psum.31 = f32[56,256]{1,0:T(8,128)} all-reduce(f32[56,256]{1,0:T(8,128)S(1)} %fusion.22), channel_id=1, replica_groups=mesh['gx'=8,'gy'=8,'ba'=4] {'gx','gy'}, use_global_device_ids=true, to_apply=%region_12.13 | all-reduce | flops 14336 | bytes 114688 | tf_op jit(solution)/shard_map/psum | solution.py:97
  (96 shorter events, 44.2 us)
Async XLA Ops:
  7.2 41.5 %copy-start.10 = (f32[56,16,128]{2,1,0:T(8,128)S(1)}, f32[56,16,128]{2,1,0:T(8,128)}, u32[]{:S(2)}) copy-start(f32[56,16,128]{2,1,0:T(8,128)} %param.4) | copy-start | bytes 1376260
  7.2 38.0 %all-gather.5.cloned.1.call-start = ((), (), s32[]{:S(2)}) async-start(), calls=%async_computation.3 | async-start | bytes 2621440 | tf_op jit(solution)/shard_map/all_gather | solution.py:78
  7.9 40.9 %copy-start.14 = (f32[56,256]{1,0:T(8,128)S(1)}, f32[56,256]{1,0:T(8,128)}, u32[]{:S(2)}) copy-start(f32[56,256]{1,0:T(8,128)} %param.5) | copy-start | bytes 172036
  7.9 172.7 %reduce-scatter.4.cloned.1.call-start = ((), (), s32[]{:S(2)}) async-start(), calls=%async_computation.4 | async-start | bytes 2621440 | tf_op jit(solution)/shard_map/reduce_scatter | solution.py:82
  52.6 164.5 %all-gather.7.cloned.1.call-start = ((), (), s32[]{:S(2)}) async-start(), calls=%async_computation.5 | async-start | bytes 2621440 | tf_op jit(solution)/shard_map/all_gather | solution.py:78
  53.9 20.4 %copy-start.15 = (s32[3]{0:T(128)S(1)}, s32[3]{0:T(128)}, u32[]{:S(2)}) copy-start(s32[3]{0:T(128)} %param.7) | copy-start | bytes 40
  53.9 16.4 %collective-permute-start = (f32[64,16,1]{2,1,0:T(8,128)S(1)}, f32[64,16,1]{2,1,0:T(8,128)S(1)}, u32[]{:S(2)}, u32[]{:S(2)}) collective-permute-start(f32[64,16,1]{2,1,0:T(8,128)S(1)} %get-tuple-element.28), channel_id=1, source_target_pairs={{0,32},{32,64},{64,96},{96,128},{128,160},{160,192},{192,224},{1,3... | collective-permute-start | bytes 12296 | tf_op jit(solution)/shard_map/ppermute | solution.py:21
  55.5 14.8 %collective-permute-start.1 = (f32[64,16,1]{2,1,0:T(8,128)S(1)}, f32[64,16,1]{2,1,0:T(8,128)S(1)}, u32[]{:S(2)}, u32[]{:S(2)}) collective-permute-start(f32[64,16,1]{2,1,0:T(8,128)S(1)} %get-tuple-element.29), channel_id=1, source_target_pairs={{32,0},{64,32},{96,64},{128,96},{160,128},{192,160},{224,192},{33,... | collective-permute-start | bytes 12296 | tf_op jit(solution)/shard_map/ppermute | solution.py:22
  70.8 17.0 %collective-permute-start.2 = (f32[64,1,130]{2,1,0:T(1,128)S(1)}, f32[64,1,130]{2,1,0:T(1,128)S(1)}, u32[]{:S(2)}, u32[]{:S(2)}) collective-permute-start(f32[64,1,130]{2,1,0:T(1,128)S(1)} %get-tuple-element.23), channel_id=1, source_target_pairs={{0,4},{4,8},{8,12},{12,16},{16,20},{20,24},{24,28},{1,5},{5,9},{9,... | collective-permute-start | bytes 99848 | tf_op jit(solution)/shard_map/ppermute | solution.py:21
  86.5 6.2 collective-permute-start.3
  93.5 1.1 copy-start.3
  186.7 33.9 %copy-start.11 = (f32[56,16,128]{2,1,0:T(8,128)S(1)}, f32[56,16,128]{2,1,0:T(8,128)}, u32[]{:S(2)}) copy-start(f32[56,16,128]{2,1,0:T(8,128)} %param.4) | copy-start | bytes 1376260
  186.7 150.9 %reduce-scatter.6.cloned.1.call-start = ((), (), s32[]{:S(2)}) async-start(), calls=%async_computation.6 | async-start | bytes 2621440 | tf_op jit(solution)/shard_map/reduce_scatter | solution.py:82
  224.6 149.2 %all-gather.9.cloned.1.call-start = ((), (), s32[]{:S(2)}) async-start(), calls=%async_computation.7 | async-start | bytes 2621440 | tf_op jit(solution)/shard_map/all_gather | solution.py:78
  225.8 3.1 collective-permute-start.4
  227.4 5.2 collective-permute-start.5
  233.1 5.3 collective-permute-start.6
  236.6 6.2 collective-permute-start.7
  243.7 1.2 copy-start.6
  333.8 1.1 copy-start.4
  343.7 33.6 %copy-start.12 = (f32[56,16,128]{2,1,0:T(8,128)S(1)}, f32[56,16,128]{2,1,0:T(8,128)}, u32[]{:S(2)}) copy-start(f32[56,16,128]{2,1,0:T(8,128)} %param.4) | copy-start | bytes 1376260
  343.7 149.7 %reduce-scatter.8.cloned.1.call-start = ((), (), s32[]{:S(2)}) async-start(), calls=%async_computation.8 | async-start | bytes 2621440 | tf_op jit(solution)/shard_map/reduce_scatter | solution.py:82
  381.3 148.3 %all-gather.11.cloned.1.call-start = ((), (), s32[]{:S(2)}) async-start(), calls=%async_computation.9 | async-start | bytes 2621440 | tf_op jit(solution)/shard_map/all_gather | solution.py:92
  382.5 3.1 collective-permute-start.8
  384.1 5.2 collective-permute-start.9
  389.3 10.1 %copy-start.7 = (f32[64,16,1]{2,1,0:T(8,128)}, f32[64,16,1]{2,1,0:T(8,128)S(1)}, u32[]{:S(2)}) copy-start(f32[64,16,1]{2,1,0:T(8,128)S(1)} %collective-permute-done.9) | copy-start | bytes 12292
  389.8 5.3 collective-permute-start.10
  393.3 6.2 collective-permute-start.11
  400.4 1.2 copy-start.5
  487.1 3.7 copy-start.8
  499.6 33.8 %copy-start.13 = (f32[56,16,128]{2,1,0:T(8,128)S(1)}, f32[56,16,128]{2,1,0:T(8,128)}, u32[]{:S(2)}) copy-start(f32[56,16,128]{2,1,0:T(8,128)} %param.4) | copy-start | bytes 1376260
  529.6 3.8 copy-start.9
  (3 other events, 3.1 us)
Sparse Core Ops, SparseCore 0:
  9.8 35.2 all-gather.4
  52.8 32.7 reduce-scatter.3
  186.9 30.1 all-gather.6
  224.7 31.9 reduce-scatter.5
  343.9 29.8 all-gather.8
  381.4 31.9 reduce-scatter.7
  499.7 29.8 all-gather.10
where the time goes:
time: 795 us; the launch traced here: 794 us
  blocking collectives  519 us (65%)
  waiting for transfers between devices  148 us (19%)
  other arithmetic  46 us (6%)
  starting transfers between devices  23.6 us (3%)
  matrix products  22.7 us (3%)
  between operations  19.1 us (2%)
  local copies, waits for them, and re-layouts  14.7 us (2%)
    psum x1, blocking collectives, local(): spectra_grad = lax.psum(partial_grad, ('gx', 'gy'))  251 us
    psum x3, blocking collectives, local(): total = lax.psum(jnp.sum(energy[:, 1:, 1:]), ('gx', 'gy', 'ba'))  245 us
    all_gather x3, waiting for transfers between devices, local(): lax.all_gather(field, 'ba', axis=0, tiled=True)  97.1 us
    all_gather x1, waiting for transfers between devices, local(): all_sparse = lax.all_gather(sparse, 'ba', axis=0, tiled=True)  30.1 us
    ppermute x6, waiting for transfers between devices, extended_2(): after = lax.ppermute(leading, axis, down)  18.8 us
  transfers between devices with their start and end apart: 19, of which 13 were waited for; matrix products, arithmetic and copies ran while one was open for 4% of the time, Pallas kernels for 0%

commit v1 on v0

--- a/solution.py
+++ b/solution.py
@@ -94,7 +94,8 @@
     partial_grad = jnp.einsum("lrc,prc->lp", resid, all_sparse, precision=HIGHEST) / math.sqrt(
         grid_rows * grid_cols
     )
-    spectra_grad = lax.psum(partial_grad, ("gx", "gy"))
+    start_zones = lambda chunk: jnp.sum(lax.all_gather(chunk, ("gx", "gy")), 0)
+    spectra_grad = start_zones(partial_grad)
     return (sparse, spectra_grad)
 
 

time: 795 us -> 628 us (0.79)
  blocking collectives: 519 us -> 268 us
  waiting for transfers between devices: 148 us -> 228 us
    psum x1 -> x0, blocking collectives: 251 us -> none  [local(): spectra_grad = lax.psum(partial_grad, ('gx', 'gy'))]
    all_gather x0 -> x1, waiting for transfers between devices: none -> 79.7 us  [local(): start_zones = lambda chunk: jnp.sum(lax.all_gather(chunk, ('gx', 'gy')), 0)]
  transfers between devices with their start and end apart: 19 -> 20, of which waited for: 13 -> 14; matrix products, arithmetic and copies ran while one was open for 4% -> 5% of each run, Pallas kernels for 0% -> 0%
where the time goes in v1:
time: 628 us; the launch traced here: 625 us
  blocking collectives  268 us (43%)
  waiting for transfers between devices  228 us (36%)
  other arithmetic  49 us (8%)
  starting transfers between devices  24 us (4%)
  matrix products  23.3 us (4%)
  between operations  18.9 us (3%)
  local copies, waits for them, and re-layouts  14.6 us (2%)
    psum x3, blocking collectives, local(): total = lax.psum(jnp.sum(energy[:, 1:, 1:]), ('gx', 'gy', 'ba'))  245 us
    all_gather x3, waiting for transfers between devices, local(): lax.all_gather(field, 'ba', axis=0, tiled=True)  97.1 us
    all_gather x1, waiting for transfers between devices, local(): start_zones = lambda chunk: jnp.sum(lax.all_gather(chunk, ('gx', 'gy')), 0)  79.7 us
    all_gather x1, waiting for transfers between devices, local(): all_sparse = lax.all_gather(sparse, 'ba', axis=0, tiled=True)  29.8 us
    ppermute x6, waiting for transfers between devices, extended_2(): after = lax.ppermute(leading, axis, down)  18.8 us
    ppermute x6, starting transfers between devices, extended_2(): before = lax.ppermute(last, axis, up)  15.2 us
  transfers between devices with their start and end apart: 20, of which 14 were waited for; matrix products, arithmetic and copies ran while one was open for 5% of the time, Pallas kernels for 0%

profile of v1, /device:TPU:2, one launch (start us, length us, event | category | flops | bytes accessed | tf_op | source)
XLA Modules:
  0.0 625.5 jit_solution(1144763333941411932)
XLA Ops:
  8.0 37.2 %all-gather.7.cloned.1.call-done = f32[256,16,128]{2,1,0:T(8,128)} async-done(((f32[64,16,128]{2,1,0:T(8,128)}), f32[256,16,128]{2,1,0:T(8,128)}) %all-gather.7.cloned.1.call-update) | async-done | bytes 2097168 | tf_op jit(solution)/shard_map/all_gather | solution.py:78
  45.1 3.5 fusion.4
  56.8 12.2 %all_gather.22 = f32[224,256]{1,0:T(8,128)S(1)} all-gather(f32[56,256]{1,0:T(8,128)S(1)} %copy-done.14), channel_id=1, replica_groups=mesh['gx'=8,'gy'=8,'ba'=4] {'ba'}, dimensions={0}, use_global_device_ids=true | all-gather | bytes 286720 | tf_op jit(solution)/shard_map/all_gather | solution.py:46
  70.7 3.5 collective-permute-start.2
  74.8 10.9 %pmax.7 = f32[]{:T(128)} all-reduce(f32[]{:T(128)} %reduce_max.9), channel_id=1, replica_groups=mesh['gx'=8,'gy'=8,'ba'=4] {'ba'}, use_global_device_ids=true, to_apply=%region_5.6 | all-reduce | flops 1 | bytes 8 | tf_op jit(solution)/shard_map/pmax | solution.py:50
  88.4 4.2 collective-permute-done.3
  96.0 78.7 %psum.21 = f32[]{:T(128)} all-reduce(f32[]{:T(128)} %slice_reduce_fusion.2), channel_id=1, replica_groups=mesh['gx'=8,'gy'=8,'ba'=4] {'gx','gy','ba'}, use_global_device_ids=true, to_apply=%region_2.0 | all-reduce | flops 1 | bytes 8 | tf_op jit(solution)/shard_map/psum | solution.py:65
  175.4 5.1 fusion.55
  180.5 6.2 fusion.45
  186.9 30.1 %all-gather.9.cloned.1.call-done = f32[256,16,128]{2,1,0:T(8,128)} async-done(((f32[64,16,128]{2,1,0:T(8,128)}), f32[256,16,128]{2,1,0:T(8,128)}) %all-gather.9.cloned.1.call-update) | async-done | bytes 2097168 | tf_op jit(solution)/shard_map/all_gather | solution.py:78
  217.0 3.5 fusion.2
  228.8 3.7 collective-permute-done.5
  233.0 3.5 collective-permute-start.6
  239.1 3.6 collective-permute-done.7
  246.1 83.2 %psum.22 = f32[]{:T(128)} all-reduce(f32[]{:T(128)} %slice_reduce_fusion.1), channel_id=1, replica_groups=mesh['gx'=8,'gy'=8,'ba'=4] {'gx','gy','ba'}, use_global_device_ids=true, to_apply=%region_8.9 | all-reduce | flops 1 | bytes 8 | tf_op jit(solution)/shard_map/psum | solution.py:65
  329.9 3.6 fusion.56
  334.7 2.7 fusion.68
  337.4 6.2 fusion.38
  343.8 29.8 %all-gather.11.cloned.1.call-done = f32[256,16,128]{2,1,0:T(8,128)} async-done(((f32[64,16,128]{2,1,0:T(8,128)}), f32[256,16,128]{2,1,0:T(8,128)}) %all-gather.11.cloned.1.call-update) | async-done | bytes 2097168 | tf_op jit(solution)/shard_map/all_gather | solution.py:78
  373.6 3.5 fusion
  385.4 3.7 collective-permute-done.9
  389.6 3.5 collective-permute-start.10
  395.7 3.6 collective-permute-done.11
  402.8 83.2 %psum.23 = f32[]{:T(128)} all-reduce(f32[]{:T(128)} %slice_reduce_fusion), channel_id=1, replica_groups=mesh['gx'=8,'gy'=8,'ba'=4] {'gx','gy','ba'}, use_global_device_ids=true, to_apply=%region_11.12 | all-reduce | flops 1 | bytes 8 | tf_op jit(solution)/shard_map/psum | solution.py:65
  486.6 3.7 fusion.57
  490.3 2.7 fusion.69
  493.0 6.1 fusion.49
  499.5 29.8 %all-gather.13.cloned.1.call-done = f32[256,16,128]{2,1,0:T(8,128)} async-done(((f32[64,16,128]{2,1,0:T(8,128)}), f32[256,16,128]{2,1,0:T(8,128)}) %all-gather.13.cloned.1.call-update) | async-done | bytes 2097168 | tf_op jit(solution)/shard_map/all_gather | solution.py:92
  529.2 3.7 fusion.6
  533.0 2.9 fusion.22
  536.0 79.7 %all-gather.15.cloned.1.call-done = f32[3584,256]{1,0:T(8,128)} async-done(((f32[56,256]{1,0:T(8,128)}), f32[3584,256]{1,0:T(8,128)}) %all-gather.15.cloned.1.call-update) | async-done | bytes 3670032 | tf_op jit(solution)/shard_map/all_gather | solution.py:97
  615.7 2.9 reduce_sum.49
  (99 shorter events, 46.4 us)
Async XLA Ops:
  7.2 41.5 %copy-start.10 = (f32[56,16,128]{2,1,0:T(8,128)S(1)}, f32[56,16,128]{2,1,0:T(8,128)}, u32[]{:S(2)}) copy-start(f32[56,16,128]{2,1,0:T(8,128)} %param.4) | copy-start | bytes 1376260
  7.2 38.0 %all-gather.7.cloned.1.call-start = ((), (), s32[]{:S(2)}) async-start(), calls=%async_computation.3 | async-start | bytes 2621440 | tf_op jit(solution)/shard_map/all_gather | solution.py:78
  7.9 40.9 %copy-start.14 = (f32[56,256]{1,0:T(8,128)S(1)}, f32[56,256]{1,0:T(8,128)}, u32[]{:S(2)}) copy-start(f32[56,256]{1,0:T(8,128)} %param.5) | copy-start | bytes 172036
  7.9 172.6 %reduce-scatter.4.cloned.1.call-start = ((), (), s32[]{:S(2)}) async-start(), calls=%async_computation.4 | async-start | bytes 2621440 | tf_op jit(solution)/shard_map/reduce_scatter | solution.py:82
  52.6 164.4 %all-gather.9.cloned.1.call-start = ((), (), s32[]{:S(2)}) async-start(), calls=%async_computation.5 | async-start | bytes 2621440 | tf_op jit(solution)/shard_map/all_gather | solution.py:78
  53.8 20.4 %copy-start.15 = (s32[3]{0:T(128)S(1)}, s32[3]{0:T(128)}, u32[]{:S(2)}) copy-start(s32[3]{0:T(128)} %param.7) | copy-start | bytes 40
  53.8 16.4 %collective-permute-start = (f32[64,16,1]{2,1,0:T(8,128)S(1)}, f32[64,16,1]{2,1,0:T(8,128)S(1)}, u32[]{:S(2)}, u32[]{:S(2)}) collective-permute-start(f32[64,16,1]{2,1,0:T(8,128)S(1)} %get-tuple-element.28), channel_id=1, source_target_pairs={{0,32},{32,64},{64,96},{96,128},{128,160},{160,192},{192,224},{1,3... | collective-permute-start | bytes 12296 | tf_op jit(solution)/shard_map/ppermute | solution.py:21
  55.5 14.8 %collective-permute-start.1 = (f32[64,16,1]{2,1,0:T(8,128)S(1)}, f32[64,16,1]{2,1,0:T(8,128)S(1)}, u32[]{:S(2)}, u32[]{:S(2)}) collective-permute-start(f32[64,16,1]{2,1,0:T(8,128)S(1)} %get-tuple-element.29), channel_id=1, source_target_pairs={{32,0},{64,32},{96,64},{128,96},{160,128},{192,160},{224,192},{33,... | collective-permute-start | bytes 12296 | tf_op jit(solution)/shard_map/ppermute | solution.py:22
  70.7 16.9 %collective-permute-start.2 = (f32[64,1,130]{2,1,0:T(1,128)S(1)}, f32[64,1,130]{2,1,0:T(1,128)S(1)}, u32[]{:S(2)}, u32[]{:S(2)}) collective-permute-start(f32[64,1,130]{2,1,0:T(1,128)S(1)} %get-tuple-element.23), channel_id=1, source_target_pairs={{0,4},{4,8},{8,12},{12,16},{16,20},{20,24},{24,28},{1,5},{5,9},{9,... | collective-permute-start | bytes 99848 | tf_op jit(solution)/shard_map/ppermute | solution.py:21
  86.4 6.2 collective-permute-start.3
  93.4 1.1 copy-start.3
  186.7 33.9 %copy-start.11 = (f32[56,16,128]{2,1,0:T(8,128)S(1)}, f32[56,16,128]{2,1,0:T(8,128)}, u32[]{:S(2)}) copy-start(f32[56,16,128]{2,1,0:T(8,128)} %param.4) | copy-start | bytes 1376260
  186.7 150.7 %reduce-scatter.6.cloned.1.call-start = ((), (), s32[]{:S(2)}) async-start(), calls=%async_computation.6 | async-start | bytes 2621440 | tf_op jit(solution)/shard_map/reduce_scatter | solution.py:82
  224.5 149.1 %all-gather.11.cloned.1.call-start = ((), (), s32[]{:S(2)}) async-start(), calls=%async_computation.7 | async-start | bytes 2621440 | tf_op jit(solution)/shard_map/all_gather | solution.py:78
  225.7 3.1 collective-permute-start.4
  227.4 5.2 collective-permute-start.5
  233.0 5.4 collective-permute-start.6
  236.5 6.2 collective-permute-start.7
  243.6 1.2 copy-start.6
  343.5 33.6 %copy-start.12 = (f32[56,16,128]{2,1,0:T(8,128)S(1)}, f32[56,16,128]{2,1,0:T(8,128)}, u32[]{:S(2)}) copy-start(f32[56,16,128]{2,1,0:T(8,128)} %param.4) | copy-start | bytes 1376260
  343.6 149.4 %reduce-scatter.8.cloned.1.call-start = ((), (), s32[]{:S(2)}) async-start(), calls=%async_computation.8 | async-start | bytes 2621440 | tf_op jit(solution)/shard_map/reduce_scatter | solution.py:82
  381.1 148.1 %all-gather.13.cloned.1.call-start = ((), (), s32[]{:S(2)}) async-start(), calls=%async_computation.9 | async-start | bytes 2621440 | tf_op jit(solution)/shard_map/all_gather | solution.py:92
  382.3 3.1 collective-permute-start.8
  384.0 5.2 collective-permute-start.9
  389.2 10.1 %copy-start.7 = (f32[64,16,1]{2,1,0:T(8,128)}, f32[64,16,1]{2,1,0:T(8,128)S(1)}, u32[]{:S(2)}) copy-start(f32[64,16,1]{2,1,0:T(8,128)S(1)} %collective-permute-done.9) | copy-start | bytes 12292
  389.6 5.4 collective-permute-start.10
  393.1 6.2 collective-permute-start.11
  400.2 1.2 copy-start.5
  486.6 3.7 copy-start.8
  499.1 33.8 %copy-start.13 = (f32[56,16,128]{2,1,0:T(8,128)S(1)}, f32[56,16,128]{2,1,0:T(8,128)}, u32[]{:S(2)}) copy-start(f32[56,16,128]{2,1,0:T(8,128)} %param.4) | copy-start | bytes 1376260
  499.2 116.6 %all-gather.15.cloned.1.call-start = ((), (), s32[]{:S(2)}) async-start(), calls=%async_computation.10 | async-start | bytes 3727360 | tf_op jit(solution)/shard_map/all_gather | solution.py:97
  529.2 3.8 copy-start.9
  (4 other events, 4.3 us)
Sparse Core Ops, SparseCore 0:
  9.8 35.2 all-gather.6
  52.7 32.7 reduce-scatter.3
  186.8 30.1 all-gather.8
  224.6 32.0 reduce-scatter.5
  343.7 29.9 all-gather.10
  381.2 32.0 reduce-scatter.7
  499.3 29.8 all-gather.12
  536.1 79.5 all-gather.14
